TPU v7x, 128 devices: a whole 4x4x4 slice. The times are simulated.
128 devices in a mesh: req: 32 (over x, z, core), seq: 4 (over y).
Axes of the slice: x: 4, y: 4, z: 4, core: 2. Of those that a mesh axis runs over, the one named last changes fastest.
Arguments:
- xs: bfloat16 [16384, 8192], P(('req', 'seq')), may hold values from -6 to 6
- bc: bfloat16 [16384, 2048], P(('req', 'seq')), may hold values from -6 to 6
- zgate: bfloat16 [16384, 8192], P(('req', 'seq'))
- dt_raw: bfloat16 [16384, 128], P(('req', 'seq'))
- dt_bias: float32 [128], replicated
- a_log: float32 [128], replicated, may hold values from -0.5 to 1
- d_skip: float32 [128], replicated, may hold values from 0.5 to 1.5
- norm_gain: float32 [8192], replicated, may hold values from 0.1 to 1.9
- resid: bfloat16 [16384, 4096], P('req', 'seq')
- w_out: bfloat16 [8192, 4096], P('req'), may hold values from -0.0625 to 0.0625
- final_gain: float32 [4096], replicated, may hold values from 0.1 to 1.9
- head_weight: bfloat16 [4096, 32768], P(None, ('req', 'seq')), may hold values from -0.09375 to 0.09375
- lengths: int32 [32, 2], P('req'), may hold values from 1 to 511, as said below
Outputs:
- layer_out: bfloat16 [16384, 4096], P('req', 'seq')
- logits: float32 [64, 32768], P(None, ('req', 'seq'))
Inputs may be any that keep to these rules, and one draw needn't show every extreme that they name: Every request has at least one row; a group's lengths sum to at most 512, and to exactly 512 in at least two groups, where one request takes all but 2 - 1 rows.
All inputs are finite; a program needn't handle non-finite values.
Results may differ from a plain program's by a relative error of at most 0.013.
Values may be sent and summed in bfloat16 or wider, within the bound.
No kernel may reach another device: no remote copies, remote signals or barrier semaphores. Data moves between devices by JAX's collectives and lax.ppermute only.
A program may use at most 128 MiB of HBM per device.

v0:
```python
import jax
import jax.numpy as jnp
from jax import lax
from jax.sharding import PartitionSpec as P

SSM_CHANNEL_COUNT = 128
HEAD_DIM = 64
NGROUPS = 8
STATE = 128


def split_halves(value):
    upper = value.astype(jnp.bfloat16)
    lower = (value - upper.astype(jnp.float32)).astype(jnp.bfloat16)
    return (upper, lower)


def group_inner(operands):
    cum_g, scores_g, inflow_g, x_g, allowed_mask = operands
    diff = cum_g[:, None, :] - cum_g[None, :, :]
    decay = jnp.where(allowed_mask[:, :, None], jnp.exp(jnp.minimum(diff, 0.0)), 0.0)
    weights = decay * scores_g[:, :, None] * inflow_g[None, :, :]
    upper, lower = split_halves(weights)
    first_part = jnp.einsum("tsk,skp->tkp", upper, x_g, preferred_element_type=jnp.float32)
    second_part = jnp.einsum("tsk,skp->tkp", lower, x_g, preferred_element_type=jnp.float32)
    return first_part + second_part


def block_terms(xb, bb, cb, dtb, segment, live, prev_seg, rate, d_skip, groups):
    rows = xb.shape[0]
    heads = rate.shape[0]
    per_group = heads // groups
    x4 = xb.reshape(rows, groups, per_group, HEAD_DIM)
    bmat = bb.reshape(rows, groups, STATE)
    cmat = cb.reshape(rows, groups, STATE)
    livef = live.astype(jnp.float32)
    cum = jnp.cumsum(-rate[None, :] * dtb, axis=0)
    inflow = dtb * livef[:, None]
    index = jnp.arange(rows, dtype=jnp.int32)
    allowed_mask = (segment[:, None] == segment[None, :]) & (index[:, None] >= index[None, :])
    scores = jnp.einsum("tgn,sgn->gts", cmat, bmat, preferred_element_type=jnp.float32)
    cum_g = cum.reshape(rows, groups, per_group).transpose(1, 0, 2)
    inflow_g = inflow.reshape(rows, groups, per_group).transpose(1, 0, 2)
    x_g = x4.transpose(1, 0, 2, 3)
    allowed_all = jnp.broadcast_to(allowed_mask[None], (groups, rows, rows))
    y_groups = lax.map(group_inner, (cum_g, scores, inflow_g, x_g, allowed_all))
    y_inner = y_groups.transpose(1, 0, 2, 3)
    skip = d_skip.reshape(1, groups, per_group, 1) * x4.astype(jnp.float32)
    last_seg = segment[rows - 1]
    tail = (
        jnp.exp(cum[rows - 1][None, :] - cum)
        * (segment == last_seg).astype(jnp.float32)[:, None]
        * inflow
    )
    scaled = tail.reshape(rows, groups, per_group, 1) * x4.astype(jnp.float32)
    upper, lower = split_halves(scaled)
    state = jnp.einsum("sgkp,sgn->gkpn", upper, bmat, preferred_element_type=jnp.float32)
    state = state + jnp.einsum("sgkp,sgn->gkpn", lower, bmat, preferred_element_type=jnp.float32)
    keep = jnp.exp(cum[rows - 1]) * (last_seg == prev_seg).astype(jnp.float32)
    carry_w = jnp.exp(cum) * (segment == prev_seg).astype(jnp.float32)[:, None]
    return (y_inner + skip, keep, state.reshape(heads, HEAD_DIM, STATE), carry_w, cmat)


def carry_term(arriving_vector, cmat, carry_w, groups):
    rows = cmat.shape[0]
    heads = arriving_vector.shape[0]
    per_group = heads // groups
    state4 = arriving_vector.reshape(groups, per_group, HEAD_DIM, STATE)
    upper, lower = split_halves(state4)
    y_carry = jnp.einsum("tgn,gkpn->tgkp", cmat, upper, preferred_element_type=jnp.float32)
    y_carry = y_carry + jnp.einsum(
        "tgn,gkpn->tgkp", cmat, lower, preferred_element_type=jnp.float32
    )
    return y_carry * carry_w.reshape(rows, groups, per_group, 1)


def gate_norm(y, zgate, norm_gain, groups):
    rows = y.shape[0]
    gated = y * jax.nn.silu(zgate.astype(jnp.float32))
    blocks = gated.reshape(rows, groups, -1)
    meansq = jnp.mean(blocks * blocks, axis=-1, keepdims=True)
    normed = (blocks * lax.rsqrt(meansq + 1e-05)).reshape(rows, -1) * norm_gain[None, :]
    return normed.astype(jnp.bfloat16)


def on_device(
    xs,
    bc,
    zgate,
    dt_raw,
    dt_bias,
    a_log,
    d_skip,
    norm_gain,
    resid,
    w_out,
    final_gain,
    head_weight,
    lengths,
):
    rows = xs.shape[0]
    inner = xs.shape[1]
    seq_count = lax.axis_size("seq")
    place = lax.axis_index("seq")
    heads_all = a_log.shape[0]
    heads = heads_all // seq_count
    groups = NGROUPS // seq_count
    share = inner // seq_count
    bshare = groups * STATE
    group_rows = rows * seq_count
    bpart = bc[:, : NGROUPS * STATE].reshape(rows, seq_count, bshare)
    cpart = bc[:, NGROUPS * STATE :].reshape(rows, seq_count, bshare)
    packed = jnp.concatenate(
        [
            xs.reshape(rows, seq_count, share),
            zgate.reshape(rows, seq_count, share),
            bpart,
            cpart,
            dt_raw.reshape(rows, seq_count, heads),
        ],
        axis=2,
    )
    moved = lax.all_to_all(packed, "seq", split_axis=1, concat_axis=0, tiled=True)
    moved = moved.reshape(group_rows, -1)
    xg = moved[:, :share]
    zg = moved[:, share : 2 * share]
    bg = moved[:, 2 * share : 2 * share + bshare]
    cg = moved[:, 2 * share + bshare : 2 * share + 2 * bshare]
    dg = moved[:, 2 * share + 2 * bshare :]
    my_heads = lambda v: lax.dynamic_slice_in_dim(v, place * heads, heads)
    rate = jnp.exp(my_heads(a_log))
    skipw = my_heads(d_skip)
    steps_dt = jax.nn.softplus(dg.astype(jnp.float32) + my_heads(dt_bias)[None, :])
    lens = lengths[0]
    slots = lens.shape[0]
    ends = jnp.cumsum(lens)
    positions = jnp.arange(group_rows, dtype=jnp.int32)
    segment = jnp.sum((positions[:, None] >= ends[None, :]).astype(jnp.int32), axis=1)
    live = segment < slots
    state_in = jnp.zeros((heads, HEAD_DIM, STATE), jnp.float32)
    prev_seg = jnp.array(-1, jnp.int32)
    ys = []
    for chunk in range(seq_count):
        lo, hi = (chunk * rows, (chunk + 1) * rows)
        local, keep, state, carry_w, cmat = block_terms(
            xg[lo:hi],
            bg[lo:hi],
            cg[lo:hi],
            steps_dt[lo:hi],
            segment[lo:hi],
            live[lo:hi],
            prev_seg,
            rate,
            skipw,
            groups,
        )
        y4 = (local + carry_term(state_in, cmat, carry_w, groups)) * live[lo:hi].astype(
            jnp.float32
        )[:, None, None, None]
        ys.append(y4.reshape(rows, share))
        state_in = keep[:, None, None] * state_in + state
        prev_seg = segment[hi - 1]
    y = jnp.concatenate(ys, axis=0)
    gain = lax.dynamic_slice_in_dim(norm_gain, place * share, share)
    gated = gate_norm(y, zg, gain, groups)
    width = resid.shape[1]
    w_cols = lax.dynamic_slice_in_dim(w_out, place * width, width, axis=1)
    w_full = lax.all_gather(w_cols, "req", axis=0, tiled=True)
    gated_all = lax.all_gather(gated, "seq", axis=1, tiled=True)
    mixer = jnp.dot(gated_all, w_full, preferred_element_type=jnp.float32).astype(jnp.bfloat16)
    layer_out = (resid.astype(jnp.float32) + mixer.astype(jnp.float32)).astype(jnp.bfloat16)
    group_pos = jnp.arange(group_rows, dtype=jnp.int32)
    picker = (group_pos[None, :] == (ends - 1)[:, None]).astype(jnp.bfloat16)
    picked_rows = jnp.dot(picker, layer_out, preferred_element_type=jnp.float32).astype(
        jnp.bfloat16
    )
    collected = lax.all_gather(picked_rows, ("req", "seq"), axis=0, tiled=True)
    owners_all = collected.shape[0] // (seq_count * slots)
    last_rows = collected.reshape(owners_all, seq_count, slots, width).transpose(0, 2, 1, 3)
    last_rows = last_rows.reshape(owners_all * slots, seq_count * width).astype(jnp.float32)
    meansq = jnp.mean(last_rows * last_rows, axis=-1, keepdims=True)
    normed = (last_rows * lax.rsqrt(meansq + 1e-05) * final_gain[None, :]).astype(jnp.bfloat16)
    logits = jnp.dot(normed, head_weight, preferred_element_type=jnp.float32)
    return (layer_out, logits)


def solution(mesh):
    placed = (
        P(("req", "seq"), None),
        P(("req", "seq"), None),
        P(("req", "seq"), None),
        P(("req", "seq"), None),
        P(),
        P(),
        P(),
        P(),
        P("req", "seq"),
        P("req", None),
        P(),
        P(None, ("req", "seq")),
        P("req", None),
    )
    return jax.shard_map(
        on_device,
        mesh=mesh,
        in_specs=placed,
        out_specs=(P("req", "seq"), P(None, ("req", "seq"))),
        check_vma=False,
    )
```

profile of v0, /device:TPU:0, one launch (start us, length us, event | category | flops | bytes accessed | tf_op | source)
XLA Modules:
  0.0 426.5 jit_solution(4121959781990282691)
XLA Ops:
  8.6 4.1 copy.339
  12.6 3.3 constant_dynamic-update-slice_fusion.4
  16.0 4.1 copy.340
  20.3 3.3 constant_dynamic-update-slice_fusion.3
  25.7 5.1 %all-to-all-start = ((bf16[128,4,4640]{0,2,1:T(8,128)(2,1)}), bf16[128,4,4640]{0,2,1:T(8,128)(2,1)}, u32[]{:S(2)}, u32[]{:S(2)}) async-start(bf16[128,4,4640]{0,2,1:T(8,128)(2,1)} %constant_dynamic-update-slice_fusion), calls=%async_computation | async-start | bytes 9502720 | tf_op jit(solution)/shard_map/all_to_all | solution.py:123
  36.4 2.5 compare_convert_fusion.7
  40.3 45.8 %all-to-all-done = bf16[128,4,4640]{0,2,1:T(8,128)(2,1)} async-done(((bf16[128,4,4640]{0,2,1:T(8,128)(2,1)}), bf16[128,4,4640]{0,2,1:T(8,128)(2,1)}, u32[]{:S(2)}, u32[]{:S(2)}) %all-to-all-start) | async-done | bytes 4751392 | tf_op jit(solution)/shard_map/all_to_all | solution.py:123
  86.0 18.4 %copy.344 = bf16[4,128,1,4640]{1,0,3,2:T(4,128)(2,1)S(1)} copy(bf16[4,128,1,4640]{1,3,0,2:T(8,128)(2,1)} %bitcast.34) | data formatting | bytes 9502720 | tf_op jit(solution)/shard_map/all_to_all | solution.py:123
  106.2 1.8 fusion.157
  114.7 1.6 reduce_window_sum.40
  116.3 1.5 copy.360
  120.2 1.5 multiply_multiply_fusion.6
  124.2 6.7 %while.40 = (s32[]{:T(128)}, f32[2,128,16,64]{1,3,2,0:T(8,128)}, bf16[2,128,16,64]{1,3,2,0:T(8,128)(2,1)S(1)}, pred[2,128,128]{2,1,0:T(8,128)(4,1)}, f32[2,128,1...) while((s32[]{:T(128)}, f32[2,128,16,64]{1,3,2,0:T(8,128)}, ...), condition=%wide.region_4.5_spmd, body=%wide.region_3.4_spmd.sunk | while | flops 71172096 | bytes 2507877 | solution.py:46
  133.8 9.1 %while.41 = (s32[]{:T(128)}, f32[2,128,16,64]{1,3,2,0:T(8,128)}, bf16[2,128,16,64]{1,3,2,0:T(8,128)(2,1)}, pred[2,128,128]{2,1,0:T(8,128)(4,1)S(1)}, f32[2,128,1...) while((s32[]{:T(128)}, f32[2,128,16,64]{1,3,2,0:T(8,128)}, ...), condition=%wide.region_7.8_spmd, body=%wide.region_6.7_spmd.sunk | while | flops 71172096 | bytes 2508385 | solution.py:46
  134.6 1.5 fusion.220
  136.1 2.3 fusion.221
  139.2 1.5 fusion.220
  140.7 2.3 fusion.221
  146.3 5.3 %while.42 = (s32[]{:T(128)}, f32[2,128,16,64]{1,3,2,0:T(8,128)}, bf16[2,128,16,64]{1,3,2,0:T(8,128)(2,1)S(1)}, pred[2,128,128]{2,1,0:T(8,128)(4,1)S(1)}, f32[2,1...) while((s32[]{:T(128)}, f32[2,128,16,64]{1,3,2,0:T(8,128)}, ...), condition=%wide.region_10.11_spmd, body=%wide.region_9.10_spmd.sunk | while | flops 71172096 | bytes 2507877 | solution.py:46
  156.7 10.6 %while.43 = (s32[]{:T(128)}, f32[2,128,16,64]{1,3,2,0:T(8,128)}, bf16[2,128,16,64]{1,3,2,0:T(8,128)(2,1)}, pred[2,128,128]{2,1,0:T(8,128)(4,1)}, f32[2,128,16]{1...) while((s32[]{:T(128)}, f32[2,128,16,64]{1,3,2,0:T(8,128)}, ...), condition=%wide.region_13.14_spmd, body=%wide.region_12.13_spmd.sunk | while | flops 71172096 | bytes 2508385 | solution.py:46
  158.1 1.5 fusion.230
  159.6 2.3 fusion.231
  163.3 1.5 fusion.230
  164.8 2.4 fusion.231
  169.9 1.6 copy.377
  179.5 2.6 bitcast_reduce_fusion
  182.2 1.8 fusion.85
  184.9 82.7 %all-gather.4.cloned.1.call-done = bf16[512,8192]{0,1:T(8,128)(2,1)} async-done(((bf16[512,2048]{0,1:T(8,128)(2,1)}), bf16[512,8192]{0,1:T(8,128)(2,1)}) %all-gather.4.cloned.1.call-update) | async-done | bytes 8388624 | tf_op jit(solution)/shard_map/all_gather | solution.py:169
  267.6 76.5 %all-gather.6.cloned.1.call-done = bf16[8192,1024]{1,0:T(8,128)(2,1)} async-done(((bf16[256,1024]{1,0:T(8,128)(2,1)}), bf16[8192,1024]{1,0:T(8,128)(2,1)}) %all-gather.6.cloned.1.call-update) | async-done | bytes 16777232 | tf_op jit(solution)/shard_map/all_gather | solution.py:168
  344.1 14.8 %add_convert_fusion = bf16[512,1024]{1,0:T(8,128)(2,1)S(1)} fusion(bf16[512,1024]{1,0:T(8,128)(2,1)S(1)} %copy-done.37, bf16[512,8192]{0,1:T(8,128)(2,1)} %all-gather.4.cloned.1.call-done, bf16[8192,1024]{1,0:T(8,128)(2,1)} %all-gather.6.cloned.1.call-done), kind=kOutput, calls=%fused_computation.111 | convolution fusion | flops 8592556032 | bytes 27262976 | tf_op jit(solution)/shard_map/dot_general | solution.py:170
  359.3 55.9 %all-gather = bf16[128,2,1024]{2,1,0:T(2,128)(2,1)S(1)} all-gather(bf16[1,2,1024]{2,1,0:T(2,128)(2,1)S(1)} %fusion.111), channel_id=1, replica_groups=mesh['req'=32,'seq'=4] {'req','seq'}, dimensions={0}, use_global_device_ids=true | all-gather | bytes 528384 | tf_op jit(solution)/shard_map/all_gather | solution.py:177
  416.9 2.7 fusion.118
  (198 shorter events, 61.7 us)
Async XLA Ops:
  7.2 176.9 %copy-start = (bf16[256,4096]{1,0:T(8,128)(2,1)S(1)}, bf16[256,4096]{1,0:T(8,128)(2,1)}, u32[]{:S(2)}) copy-start(bf16[256,4096]{1,0:T(8,128)(2,1)} %param.30) | copy-start | bytes 6291460
  12.6 7.5 %copy-start.23 = (bf16[128,128]{1,0:T(8,128)(2,1)S(1)}, bf16[128,128]{1,0:T(8,128)(2,1)}, u32[]{:S(2)}) copy-start(bf16[128,128]{1,0:T(8,128)(2,1)} %param.24) | copy-start | bytes 98308
  25.7 5.2 %copy-start.38 = (s32[1,2]{1,0:T(1,128)S(1)}, s32[1,2]{1,0:T(1,128)}, u32[]{:S(2)}) copy-start(s32[1,2]{1,0:T(1,128)} %param.33) | copy-start | bytes 28
  25.7 9.1 %copy-start.39 = (f32[128]{0:T(128)S(1)}, f32[128]{0:T(128)}, u32[]{:S(2)}) copy-start(f32[128]{0:T(128)} %param.25) | copy-start | bytes 1540
  25.7 9.2 %copy-start.40 = (f32[128]{0:T(128)S(1)}, f32[128]{0:T(128)}, u32[]{:S(2)}) copy-start(f32[128]{0:T(128)} %param.27) | copy-start | bytes 1540
  25.7 10.0 %copy-start.41 = (f32[128]{0:T(128)S(1)}, f32[128]{0:T(128)}, u32[]{:S(2)}) copy-start(f32[128]{0:T(128)} %param.26) | copy-start | bytes 1540
  25.7 60.3 %all-to-all-start = ((bf16[128,4,4640]{0,2,1:T(8,128)(2,1)}), bf16[128,4,4640]{0,2,1:T(8,128)(2,1)}, u32[]{:S(2)}, u32[]{:S(2)}) async-start(bf16[128,4,4640]{0,2,1:T(8,128)(2,1)} %constant_dynamic-update-slice_fusion), calls=%async_computation | async-start | bytes 9502720 | tf_op jit(solution)/shard_map/all_to_all | solution.py:123
  30.9 236.8 %all-gather.4.cloned.1.call-start = ((), (), s32[]{:S(2)}) async-start(), calls=%async_computation.1 | async-start | bytes 10485760 | tf_op jit(solution)/shard_map/all_gather | solution.py:169
  31.1 73.3 %copy-start.34 = (s32[2,1]{0,1:T(1,128)}, s32[2,1]{0,1:T(1,128)S(1)}, u32[]{:S(2)}) copy-start(s32[2,1]{0,1:T(1,128)S(1)} %reduce-window.7) | copy-start | bytes 28
  105.3 2.7 copy-start.1
  106.2 24.7 %copy-start.8 = (bf16[128,256]{0,1:T(8,128)(2,1)}, bf16[128,256]{0,1:T(8,128)(2,1)S(1)}, u32[]{:S(2)}) copy-start(bf16[128,256]{0,1:T(8,128)(2,1)S(1)} %get-tuple-element.281) | copy-start | bytes 196612
  106.2 38.1 %copy-start.10 = (bf16[128,256]{0,1:T(8,128)(2,1)}, bf16[128,256]{0,1:T(8,128)(2,1)S(1)}, u32[]{:S(2)}) copy-start(bf16[128,256]{0,1:T(8,128)(2,1)S(1)} %get-tuple-element.278) | copy-start | bytes 196612
  108.1 11.0 %copy-start.15 = (f32[512,32]{0,1:T(8,128)}, f32[512,32]{0,1:T(8,128)S(1)}, u32[]{:S(2)}) copy-start(f32[512,32]{0,1:T(8,128)S(1)} %compare_select_fusion) | copy-start | bytes 196612
  133.8 12.4 %copy-start.17 = (f32[128,32]{0,1:T(8,128)S(1)}, f32[128,32]{0,1:T(8,128)}, u32[]{:S(2)}) copy-start(f32[128,32]{0,1:T(8,128)} %copy.360) | copy-start | bytes 49156
  146.3 5.3 %copy-start.36 = (f32[32]{0:T(128)S(1)}, f32[32]{0:T(128)}, u32[]{:S(2)}) copy-start(f32[32]{0:T(128)} %get-tuple-element.325) | copy-start | bytes 388
  146.3 5.9 %copy-start.22 = (f32[128,32]{0,1:T(8,128)S(1)}, f32[128,32]{0,1:T(8,128)}, u32[]{:S(2)}) copy-start(f32[128,32]{0,1:T(8,128)} %get-tuple-element.289) | copy-start | bytes 49156
  167.2 7.4 %copy-start.9 = (bf16[128,256]{0,1:T(8,128)(2,1)S(1)}, bf16[128,256]{0,1:T(8,128)(2,1)}, u32[]{:S(2)}) copy-start(bf16[128,256]{0,1:T(8,128)(2,1)} %copy-done.8) | copy-start | bytes 196612
  169.9 5.0 %copy-start.12 = (bf16[128,256]{0,1:T(8,128)(2,1)S(1)}, bf16[128,256]{0,1:T(8,128)(2,1)}, u32[]{:S(2)}) copy-start(bf16[128,256]{0,1:T(8,128)(2,1)} %get-tuple-element.280) | copy-start | bytes 196612
  169.9 5.0 %copy-start.20 = (f32[128,32]{0,1:T(8,128)S(1)}, f32[128,32]{0,1:T(8,128)}, u32[]{:S(2)}) copy-start(f32[128,32]{0,1:T(8,128)} %get-tuple-element.300) | copy-start | bytes 49156
  169.9 5.3 %copy-start.32 = (f32[2,16]{1,0:T(2,128)S(1)}, f32[2,16]{1,0:T(2,128)}, u32[]{:S(2)}) copy-start(f32[2,16]{1,0:T(2,128)} %mul.517) | copy-start | bytes 388
  171.5 3.4 copy-start.2
  176.9 1.4 copy-start.5
  176.9 1.3 copy-start.27
  177.6 1.4 copy-start.7
  177.6 1.4 copy-start.21
  177.6 1.4 copy-start.26
  179.4 2.7 dynamic-slice-start
  182.1 2.8 copy-start.35
  182.1 162.0 %copy-start.37 = (bf16[512,1024]{1,0:T(8,128)(2,1)S(1)}, bf16[512,1024]{1,0:T(8,128)(2,1)}, u32[]{:S(2)}) copy-start(bf16[512,1024]{1,0:T(8,128)(2,1)} %param.29) | copy-start | bytes 3145732
  184.0 160.1 %all-gather.6.cloned.1.call-start = ((), (), s32[]{:S(2)}) async-start(), calls=%async_computation.2 | async-start | bytes 17301504 | tf_op jit(solution)/shard_map/all_gather | solution.py:168
  359.0 57.7 %copy-start.13 = (bf16[512,1024]{1,0:T(8,128)(2,1)}, bf16[512,1024]{1,0:T(8,128)(2,1)S(1)}, u32[]{:S(2)}) copy-start(bf16[512,1024]{1,0:T(8,128)(2,1)S(1)} %add_convert_fusion) | copy-start | bytes 3145732
  359.0 57.9 %copy-start.24 = (f32[4096]{0:T(1024)S(1)}, f32[4096]{0:T(1024)}, u32[]{:S(2)}) copy-start(f32[4096]{0:T(1024)} %param.31) | copy-start | bytes 49156
  (14 other events, 16.7 us)
Sparse Core Ops, SparseCore 0:
  184.1 83.4 all-gather.3
  270.5 73.5 all-gather.5
where the time goes:
time: 429 us; the launch traced here: 426 us
  waiting for transfers between devices  205 us (48%)
  local copies, waits for them, and re-layouts  71.9 us (17%)
  blocking collectives  55.9 us (13%)
  matrix products  50.2 us (12%)
  other arithmetic  20.6 us (5%)
  between operations  17.7 us (4%)
  starting transfers between devices  5.2 us (1%)
    all_gather x1, waiting for transfers between devices, on_device(): gated_all = lax.all_gather(gated, 'seq', axis=1, tiled=True)  82.7 us
    all_gather x1, waiting for transfers between devices, on_device(): w_full = lax.all_gather(w_cols, 'req', axis=0, tiled=True)  76.5 us
    all_gather x1, blocking collectives, on_device(): collected = lax.all_gather(picked_rows, ('req', 'seq'), axis=0, tiled=True)  55.9 us
    all_to_all x1, waiting for transfers between devices, on_device(): lax.all_to_all(packed, 'seq', split_axis=1, concat_axis=0, tiled=True)  45.8 us
    unnamed x93, local copies, waits for them, and re-layouts  18.8 us
    all_to_all x1, local copies, waits for them, and re-layouts, on_device(): lax.all_to_all(packed, 'seq', split_axis=1, concat_axis=0, tiled=True)  18.4 us
    dot_general x8, matrix products, group_inner(): jnp.einsum('tsk,skp->tkp', lower, x_g, preferred_element_type=jnp.float32)  14.9 us
    dot_general x1, matrix products, on_device(): jnp.dot(gated_all, w_full, preferred_element_type=jnp.float32)  14.8 us
  transfers between devices with their start and end apart: 3, of which 3 were waited for; matrix products, arithmetic and copies ran while one was open for 2% of the time, Pallas kernels for 0%

commit v1 on v0

--- a/solution.py
+++ b/solution.py
@@ -7,6 +7,28 @@
 HEAD_DIM = 64
 NGROUPS = 8
 STATE = 128
+
+
+def joined_along(parts, dim):
+    parts = jnp.moveaxis(parts, 0, dim)
+    lengths = parts.shape
+    return parts.reshape(*lengths[:dim], lengths[dim] * lengths[dim + 1], *lengths[dim + 2 :])
+
+
+def collect(value, axis, dim):
+    size = lax.axis_size(axis)
+    pairs = [(i, (i + 1) % size) for i in range(size)]
+    back = [(b, a) for a, b in pairs]
+    lower, upper = ([], [])
+    for step in range(size - 1):
+        if step % 2 == 0:
+            lower.append(lax.ppermute(lower[-1] if lower else value, axis, pairs))
+        else:
+            upper.append(lax.ppermute(upper[-1] if upper else value, axis, back))
+    blocks = jnp.stack([*lower[::-1], value, *upper])
+    shift = lax.axis_index(axis) - len(lower)
+    blocks = blocks[(jnp.arange(size) - shift) % size]
+    return joined_along(blocks, dim)
 
 
 def split_halves(value):
@@ -166,7 +188,7 @@
     width = resid.shape[1]
     w_cols = lax.dynamic_slice_in_dim(w_out, place * width, width, axis=1)
     w_full = lax.all_gather(w_cols, "req", axis=0, tiled=True)
-    gated_all = lax.all_gather(gated, "seq", axis=1, tiled=True)
+    gated_all = collect(gated, "seq", 1)
     mixer = jnp.dot(gated_all, w_full, preferred_element_type=jnp.float32).astype(jnp.bfloat16)
     layer_out = (resid.astype(jnp.float32) + mixer.astype(jnp.float32)).astype(jnp.bfloat16)
     group_pos = jnp.arange(group_rows, dtype=jnp.int32)

time: 429 us -> 390 us (0.909)
  waiting for transfers between devices: 205 us -> 139 us
  matrix products: 50.2 us -> 66.7 us
  local copies, waits for them, and re-layouts: 71.9 us -> 77 us
    ppermute x0 -> x3, waiting for transfers between devices: none -> 91.9 us  [the longest x2 91.9 us: collect(): lower.append(lax.ppermute(lower[-1] if lower else value, axis, pairs))]
    all_gather x1 -> x0, waiting for transfers between devices: 82.7 us -> none  [on_device(): gated_all = lax.all_gather(gated, 'seq', axis=1, tiled=True)]
    all_gather x1, waiting for transfers between devices: 76.5 us -> 0.01 us  [on_device(): w_full = lax.all_gather(w_cols, 'req', axis=0, tiled=True)]
    gather x0 -> x3, local copies, waits for them, and re-layouts: none -> 13.6 us  [collect(): blocks = blocks[(jnp.arange(size) - shift) % size]]
    unnamed x0 -> x1, other arithmetic: none -> 7.36 us
    dot_general x3, matrix products: 1.19 us -> 8 us  [carry_term(): jnp.einsum('tgn,gkpn->tgkp', cmat, lower, preferred_element_type=jnp.floa...]
    dot_general x4, matrix products: 1.19 us -> 6.59 us  [carry_term(): jnp.einsum('tgn,gkpn->tgkp', cmat, upper, preferred_element_type=jnp.floa...]
    unnamed x93 -> x99, local copies, waits for them, and re-layouts: 18.8 us -> 19.6 us
  transfers between devices with their start and end apart: 3 -> 5, of which waited for: 3 -> 3; matrix products, arithmetic and copies ran while one was open for 2% -> 36% of each run, Pallas kernels for 0% -> 0%
where the time goes in v1:
time: 390 us; the launch traced here: 387 us
  waiting for transfers between devices  139 us (36%)
  local copies, waits for them, and re-layouts  77 us (20%)
  matrix products  66.7 us (17%)
  blocking collectives  56.4 us (14%)
  other arithmetic  21.7 us (6%)
  between operations  17.9 us (5%)
  starting transfers between devices  8.45 us (2%)
    ppermute x2, waiting for transfers between devices, collect(): lower.append(lax.ppermute(lower[-1] if lower else value, axis, pairs))  91.9 us
    all_gather x1, blocking collectives, on_device(): collected = lax.all_gather(picked_rows, ('req', 'seq'), axis=0, tiled=True)  56.4 us
    all_to_all x1, waiting for transfers between devices, on_device(): lax.all_to_all(packed, 'seq', split_axis=1, concat_axis=0, tiled=True)  46.8 us
    unnamed x99, local copies, waits for them, and re-layouts  19.6 us
    dot_general x8, matrix products, group_inner(): jnp.einsum('tsk,skp->tkp', lower, x_g, preferred_element_type=jnp.float32)  18.9 us
    all_to_all x1, local copies, waits for them, and re-layouts, on_device(): lax.all_to_all(packed, 'seq', split_axis=1, concat_axis=0, tiled=True)  18.4 us
    dot_general x1, matrix products, on_device(): jnp.dot(gated_all, w_full, preferred_element_type=jnp.float32)  14.9 us
    gather x3, local copies, waits for them, and re-layouts, collect(): blocks = blocks[(jnp.arange(size) - shift) % size]  13.6 us
  transfers between devices with their start and end apart: 5, of which 3 were waited for; matrix products, arithmetic and copies ran while one was open for 36% of the time, Pallas kernels for 0%

profile of v1, /device:TPU:0, one launch (start us, length us, event | category | flops | bytes accessed | tf_op | source)
XLA Modules:
  0.0 387.2 jit_solution(12070511470077543668)
XLA Ops:
  10.9 4.1 %copy.344 = bf16[128,8192]{0,1:T(8,128)(2,1)} copy(bf16[128,8192]{1,0:T(8,128)(2,1)} %param.21) | data formatting | bytes 4194304 | tf_op args[0]
  15.0 3.2 copy.345
  18.5 3.3 constant_dynamic-update-slice_fusion.4
  25.7 5.1 %all-to-all-start = ((bf16[128,4,4640]{0,2,1:T(8,128)(2,1)}), bf16[128,4,4640]{0,2,1:T(8,128)(2,1)}, u32[]{:S(2)}, u32[]{:S(2)}) async-start(bf16[128,4,4640]{0,2,1:T(8,128)(2,1)} %constant_dynamic-update-slice_fusion), calls=%async_computation | async-start | bytes 9502720 | tf_op jit(solution)/shard_map/all_to_all | solution.py:145
  39.2 46.8 %all-to-all-done = bf16[128,4,4640]{0,2,1:T(8,128)(2,1)} async-done(((bf16[128,4,4640]{0,2,1:T(8,128)(2,1)}), bf16[128,4,4640]{0,2,1:T(8,128)(2,1)}, u32[]{:S(2)}, u32[]{:S(2)}) %all-to-all-start) | async-done | bytes 4751392 | tf_op jit(solution)/shard_map/all_to_all | solution.py:145
  86.0 18.4 %copy.349 = bf16[4,128,1,4640]{1,0,3,2:T(4,128)(2,1)S(1)} copy(bf16[4,128,1,4640]{1,3,0,2:T(8,128)(2,1)} %bitcast.34) | data formatting | bytes 9502720 | tf_op jit(solution)/shard_map/all_to_all | solution.py:145
  115.9 2.5 fusion.160
  126.0 12.2 %while.40 = (s32[]{:T(128)}, f32[2,128,16,64]{1,3,2,0:T(8,128)}, bf16[2,128,16,64]{1,3,2,0:T(8,128)(2,1)}, pred[2,128,128]{2,1,0:T(8,128)(4,1)}, f32[2,128,16]{1...) while((s32[]{:T(128)}, f32[2,128,16,64]{1,3,2,0:T(8,128)}, ...), condition=%wide.region_4.5_spmd, body=%wide.region_3.4_spmd.sunk | while | flops 71172096 | bytes 2508385 | solution.py:68
  129.8 2.4 fusion.219
  135.9 2.4 fusion.219
  138.3 2.8 fusion.89
  143.6 10.6 %while.41 = (s32[]{:T(128)}, f32[2,128,16,64]{1,3,2,0:T(8,128)}, bf16[2,128,16,64]{1,3,2,0:T(8,128)(2,1)}, pred[2,128,128]{2,1,0:T(8,128)(4,1)}, f32[2,128,16]{1...) while((s32[]{:T(128)}, f32[2,128,16,64]{1,3,2,0:T(8,128)}, ...), condition=%wide.region_7.8_spmd, body=%wide.region_6.7_spmd.sunk | while | flops 71172096 | bytes 2508385 | solution.py:68
  151.8 2.4 fusion.224
  154.2 3.1 fusion.103
  158.5 8.1 %while.42 = (s32[]{:T(128)}, f32[2,128,16,64]{1,3,2,0:T(8,128)}, bf16[2,128,16,64]{1,3,2,0:T(8,128)(2,1)}, pred[2,128,128]{2,1,0:T(8,128)(4,1)S(1)}, f32[2,128,1...) while((s32[]{:T(128)}, f32[2,128,16,64]{1,3,2,0:T(8,128)}, ...), condition=%wide.region_10.11_spmd, body=%wide.region_9.10_spmd.sunk | while | flops 71172096 | bytes 2508385 | solution.py:68
  164.2 2.4 fusion.229
  166.6 2.7 fusion.98
  170.6 7.8 %while.43 = (s32[]{:T(128)}, f32[2,128,16,64]{1,3,2,0:T(8,128)}, bf16[2,128,16,64]{1,3,2,0:T(8,128)(2,1)}, pred[2,128,128]{2,1,0:T(8,128)(4,1)S(1)}, f32[2,128,1...) while((s32[]{:T(128)}, f32[2,128,16,64]{1,3,2,0:T(8,128)}, ...), condition=%wide.region_13.14_spmd, body=%wide.region_12.13_spmd.sunk | while | flops 71172096 | bytes 2508385 | solution.py:68
  172.2 2.4 fusion.234
  176.1 2.4 fusion.234
  181.1 2.6 bitcast_reduce_fusion
  184.9 2.6 collective-permute-start.2
  187.5 44.7 %collective-permute-done = bf16[512,2048]{0,1:T(8,128)(2,1)} collective-permute-done((bf16[512,2048]{0,1:T(8,128)(2,1)S(1)}, bf16[512,2048]{0,1:T(8,128)(2,1)}, u32[]{:S(2)}, u32[]{:S(2)}) %collective-permute-start) | collective-permute-done | bytes 2097184 | tf_op jit(solution)/shard_map/ppermute | solution.py:25
  232.2 47.2 %collective-permute-done.1 = bf16[512,2048]{0,1:T(8,128)(2,1)} collective-permute-done((bf16[512,2048]{0,1:T(8,128)(2,1)}, bf16[512,2048]{0,1:T(8,128)(2,1)}, u32[]{:S(2)}, u32[]{:S(2)}) %collective-permute-start.1) | collective-permute-done | bytes 2097184 | tf_op jit(solution)/shard_map/ppermute | solution.py:25
  279.4 3.8 pad_maximum_fusion
  283.2 3.6 fusion.158
  286.9 5.0 %gather_fusion = bf16[4,512,1024]{1,2,0:T(8,128)(2,1)} fusion(bf16[4,512,1024]{1,2,0:T(8,128)(2,1)} %get-tuple-element.275, s32[1024]{0:T(1024)S(1)} %pad_clamp_fusion), kind=kCustom, calls=%fused_computation | custom fusion | bytes 8388624 | tf_op jit(solution)/shard_map/gather | solution.py:30
  291.9 5.0 %gather_fusion.1 = bf16[4,512,1024]{1,2,0:T(8,128)(2,1)} fusion(bf16[4,512,1024]{1,2,0:T(8,128)(2,1)} %get-tuple-element.276, s32[1024]{0:T(1024)S(1)} %pad_clamp_fusion), kind=kCustom, calls=%fused_computation.1 | custom fusion | bytes 8388624 | tf_op jit(solution)/shard_map/gather | solution.py:30
  296.9 7.4 %pad_maximum_fusion.1 = bf16[4,512,2048]{1,2,0:T(8,128)(2,1)} fusion(bf16[4,512,1024]{1,2,0:T(8,128)(2,1)} %gather_fusion.1, bf16[4,512,1024]{1,2,0:T(8,128)(2,1)} %gather_fusion), kind=kLoop, calls=%fused_computation.103 | loop fusion | flops 16777216 | bytes 16777216
  304.2 14.9 %add_convert_fusion = bf16[512,1024]{1,0:T(8,128)(2,1)S(1)} fusion(bf16[512,1024]{1,0:T(8,128)(2,1)S(1)} %copy-done.40, bf16[512,8192]{0,1:T(8,128)(2,1)} %bitcast.334, bf16[8192,1024]{1,0:T(8,128)(2,1)} %all-gather.3.cloned.1.call-done), kind=kOutput, calls=%fused_computation.115 | convolution fusion | flops 8592556032 | bytes 27262976 | tf_op jit(solution)/shard_map/dot_general | solution.py:192
  319.4 56.4 %all-gather = bf16[128,2,1024]{2,1,0:T(2,128)(2,1)S(1)} all-gather(bf16[1,2,1024]{2,1,0:T(2,128)(2,1)S(1)} %fusion.111), channel_id=1, replica_groups=mesh['req'=32,'seq'=4] {'req','seq'}, dimensions={0}, use_global_device_ids=true | all-gather | bytes 528384 | tf_op jit(solution)/shard_map/all_gather | solution.py:199
  377.6 2.7 fusion.118
  (214 shorter events, 66.9 us)
Async XLA Ops:
  7.2 297.0 %all-gather.3.cloned.1.call-start = ((), (), s32[]{:S(2)}) async-start(), calls=%async_computation.1 | async-start | bytes 17301504 | tf_op jit(solution)/shard_map/all_gather | solution.py:190
  10.9 7.5 %copy-start.29 = (bf16[128,128]{1,0:T(8,128)(2,1)S(1)}, bf16[128,128]{1,0:T(8,128)(2,1)}, u32[]{:S(2)}) copy-start(bf16[128,128]{1,0:T(8,128)(2,1)} %param.24) | copy-start | bytes 98308
  25.7 5.1 %copy-start.41 = (s32[1,2]{1,0:T(1,128)S(1)}, s32[1,2]{1,0:T(1,128)}, u32[]{:S(2)}) copy-start(s32[1,2]{1,0:T(1,128)} %param.33) | copy-start | bytes 28
  25.7 9.2 %copy-start.42 = (f32[128]{0:T(128)S(1)}, f32[128]{0:T(128)}, u32[]{:S(2)}) copy-start(f32[128]{0:T(128)} %param.25) | copy-start | bytes 1540
  25.7 9.3 %copy-start.43 = (f32[128]{0:T(128)S(1)}, f32[128]{0:T(128)}, u32[]{:S(2)}) copy-start(f32[128]{0:T(128)} %param.27) | copy-start | bytes 1540
  25.7 10.0 %copy-start.44 = (f32[128]{0:T(128)S(1)}, f32[128]{0:T(128)}, u32[]{:S(2)}) copy-start(f32[128]{0:T(128)} %param.26) | copy-start | bytes 1540
  25.7 60.3 %all-to-all-start = ((bf16[128,4,4640]{0,2,1:T(8,128)(2,1)}), bf16[128,4,4640]{0,2,1:T(8,128)(2,1)}, u32[]{:S(2)}, u32[]{:S(2)}) async-start(bf16[128,4,4640]{0,2,1:T(8,128)(2,1)} %constant_dynamic-update-slice_fusion), calls=%async_computation | async-start | bytes 9502720 | tf_op jit(solution)/shard_map/all_to_all | solution.py:145
  35.8 76.8 %copy-start.32 = (f32[128]{0:T(128)}, f32[128]{0:T(128)S(1)}, u32[]{:S(2)}) copy-start(f32[128]{0:T(128)S(1)} %get-tuple-element.320) | copy-start | bytes 1540
  35.8 76.8 %copy-start.34 = (f32[128]{0:T(128)}, f32[128]{0:T(128)S(1)}, u32[]{:S(2)}) copy-start(f32[128]{0:T(128)S(1)} %get-tuple-element.321) | copy-start | bytes 1540
  35.8 76.8 %copy-start.35 = (f32[128]{0:T(128)}, f32[128]{0:T(128)S(1)}, u32[]{:S(2)}) copy-start(f32[128]{0:T(128)S(1)} %get-tuple-element.322) | copy-start | bytes 1540
  35.8 76.8 %copy-start.36 = (f32[128]{0:T(128)}, f32[128]{0:T(128)S(1)}, u32[]{:S(2)}) copy-start(f32[128]{0:T(128)S(1)} %get-tuple-element.323) | copy-start | bytes 1540
  108.4 10.4 %copy-start.19 = (f32[128,32]{0,1:T(8,128)}, f32[128,32]{0,1:T(8,128)S(1)}, u32[]{:S(2)}) copy-start(f32[128,32]{0,1:T(8,128)S(1)} %copy.356) | copy-start | bytes 49156
  108.6 10.1 %copy-start.17 = (f32[128,32]{0,1:T(8,128)}, f32[128,32]{0,1:T(8,128)S(1)}, u32[]{:S(2)}) copy-start(f32[128,32]{0,1:T(8,128)S(1)} %copy.365) | copy-start | bytes 49156
  114.3 5.4 %copy-start.14 = (bf16[128,256]{0,1:T(8,128)(2,1)}, bf16[128,256]{0,1:T(8,128)(2,1)S(1)}, u32[]{:S(2)}) copy-start(bf16[128,256]{0,1:T(8,128)(2,1)S(1)} %get-tuple-element.283) | copy-start | bytes 196612
  114.4 7.0 %copy-start.12 = (bf16[128,256]{0,1:T(8,128)(2,1)}, bf16[128,256]{0,1:T(8,128)(2,1)S(1)}, u32[]{:S(2)}) copy-start(bf16[128,256]{0,1:T(8,128)(2,1)S(1)} %get-tuple-element.281) | copy-start | bytes 196612
  114.4 8.6 %copy-start.10 = (bf16[128,256]{0,1:T(8,128)(2,1)}, bf16[128,256]{0,1:T(8,128)(2,1)S(1)}, u32[]{:S(2)}) copy-start(bf16[128,256]{0,1:T(8,128)(2,1)S(1)} %get-tuple-element.279) | copy-start | bytes 196612
  143.6 10.6 %copy-start.25 = (f32[128,2,16]{0,2,1:T(8,128)S(1)}, f32[128,2,16]{0,2,1:T(8,128)}, u32[]{:S(2)}) copy-start(f32[128,2,16]{0,2,1:T(8,128)} %get-tuple-element.325) | copy-start | bytes 49156
  158.5 8.1 %copy-start.9 = (f32[2,16,64,128]{3,2,1,0:T(8,128)S(1)}, f32[2,16,64,128]{3,2,1,0:T(8,128)}, u32[]{:S(2)}) copy-start(f32[2,16,64,128]{3,2,1,0:T(8,128)} %fusion.140) | copy-start | bytes 3145732
  158.5 8.1 %copy-start.13 = (bf16[128,256]{0,1:T(8,128)(2,1)S(1)}, bf16[128,256]{0,1:T(8,128)(2,1)}, u32[]{:S(2)}) copy-start(bf16[128,256]{0,1:T(8,128)(2,1)} %copy-done.12) | copy-start | bytes 196612
  158.5 8.1 %copy-start.24 = (f32[128,2,16]{0,2,1:T(8,128)S(1)}, f32[128,2,16]{0,2,1:T(8,128)}, u32[]{:S(2)}) copy-start(f32[128,2,16]{0,2,1:T(8,128)} %get-tuple-element.324) | copy-start | bytes 49156
  170.6 7.9 %copy-start.11 = (bf16[128,256]{0,1:T(8,128)(2,1)S(1)}, bf16[128,256]{0,1:T(8,128)(2,1)}, u32[]{:S(2)}) copy-start(bf16[128,256]{0,1:T(8,128)(2,1)} %copy-done.10) | copy-start | bytes 196612
  170.6 7.9 %copy-start.23 = (f32[128,2,16]{0,2,1:T(8,128)S(1)}, f32[128,2,16]{0,2,1:T(8,128)}, u32[]{:S(2)}) copy-start(f32[128,2,16]{0,2,1:T(8,128)} %copy.382) | copy-start | bytes 49156
  170.6 7.9 %copy-start.31 = (f32[2,16]{1,0:T(2,128)S(1)}, f32[2,16]{1,0:T(2,128)}, u32[]{:S(2)}) copy-start(f32[2,16]{1,0:T(2,128)} %mul.481) | copy-start | bytes 388
  170.6 7.9 %copy-start.33 = (f32[128]{0:T(128)S(1)}, f32[128]{0:T(128)}, u32[]{:S(2)}) copy-start(f32[128]{0:T(128)} %copy-done.32) | copy-start | bytes 1540
  183.7 48.5 %copy-start.39 = (s32[2,1]{0,1:T(1,128)S(1)}, s32[2,1]{0,1:T(1,128)}, u32[]{:S(2)}) copy-start(s32[2,1]{0,1:T(1,128)} %copy-done.38) | copy-start | bytes 28
  184.2 48.0 %collective-permute-start = (bf16[512,2048]{0,1:T(8,128)(2,1)S(1)}, bf16[512,2048]{0,1:T(8,128)(2,1)}, u32[]{:S(2)}, u32[]{:S(2)}) collective-permute-start(bf16[512,2048]{0,1:T(8,128)(2,1)S(1)} %fusion.85), channel_id=1, source_target_pairs={{0,1},{1,2},{2,3},{3,0},{4,5},{5,6},{6,7},{7,4},{8,9},{9,10},{10,1... | collective-permute-start | bytes 6291464 | tf_op jit(solution)/shard_map/ppermute | solution.py:25
  184.9 47.3 %collective-permute-start.2 = (bf16[512,2048]{0,1:T(8,128)(2,1)S(1)}, bf16[512,2048]{0,1:T(8,128)(2,1)}, u32[]{:S(2)}, u32[]{:S(2)}) collective-permute-start(bf16[512,2048]{0,1:T(8,128)(2,1)S(1)} %fusion.85), channel_id=1, source_target_pairs={{1,0},{2,1},{3,2},{0,3},{5,4},{6,5},{7,6},{4,7},{9,8},{10,9},{11,1... | collective-permute-start | bytes 6291464 | tf_op jit(solution)/shard_map/ppermute | solution.py:27
  232.1 47.3 %collective-permute-start.1 = (bf16[512,2048]{0,1:T(8,128)(2,1)}, bf16[512,2048]{0,1:T(8,128)(2,1)}, u32[]{:S(2)}, u32[]{:S(2)}) collective-permute-start(bf16[512,2048]{0,1:T(8,128)(2,1)} %collective-permute-done), channel_id=1, source_target_pairs={{0,1},{1,2},{2,3},{3,0},{4,5},{5,6},{6,7},{7,4},{8,9},{9,10},{10,1... | collective-permute-start | bytes 6291464 | tf_op jit(solution)/shard_map/ppermute | solution.py:25
  296.9 7.4 %copy-start.40 = (bf16[512,1024]{1,0:T(8,128)(2,1)S(1)}, bf16[512,1024]{1,0:T(8,128)(2,1)}, u32[]{:S(2)}) copy-start(bf16[512,1024]{1,0:T(8,128)(2,1)} %param.29) | copy-start | bytes 3145732
  319.1 58.3 %copy-start.15 = (bf16[512,1024]{1,0:T(8,128)(2,1)}, bf16[512,1024]{1,0:T(8,128)(2,1)S(1)}, u32[]{:S(2)}) copy-start(bf16[512,1024]{1,0:T(8,128)(2,1)S(1)} %add_convert_fusion) | copy-start | bytes 3145732
  319.1 58.5 %copy-start.30 = (f32[4096]{0:T(1024)S(1)}, f32[4096]{0:T(1024)}, u32[]{:S(2)}) copy-start(f32[4096]{0:T(1024)} %param.31) | copy-start | bytes 49156
  319.1 61.2 %copy-start.1 = (bf16[256,4096]{1,0:T(8,128)(2,1)S(1)}, bf16[256,4096]{1,0:T(8,128)(2,1)}, u32[]{:S(2)}) copy-start(bf16[256,4096]{1,0:T(8,128)(2,1)} %param.30) | copy-start | bytes 6291460
  (19 other events, 60.7 us)
Sparse Core Ops, SparseCore 0:
  10.2 75.1 all-gather.2
